TPU v7x, 32 devices: a whole 2x2x4 slice. The times are simulated.
32 devices in a mesh: row: 8 (over z, core), col: 4 (over y, x).
Axes of the slice: x: 2, y: 2, z: 4, core: 2. Of those that a mesh axis runs over, the one named last changes fastest.
Arguments:
- trunk_in: bfloat16 [1536, 8192], P('col', 'row'), may hold values from -24 to 24
- conv_weight: bfloat16 [5, 1536, 1536], P(None, 'col'), may hold values from -0.0625 to 0.0625
- conv_bias: float32 [1536], P('col'), may hold values from -3 to 3
- norm_gain: float32 [1536], replicated, may hold values from 0.1 to 1.9
- pair_proj: bfloat16 [64, 1536], replicated, may hold values from -0.15625 to 0.15625
- pair_in: bfloat16 [512, 128, 128], P('row', 'col'), may hold values from -6 to 6
- opm_weight: bfloat16 [1024, 128], replicated, may hold values from -0.1875 to 0.1875
- pair_bias: float32 [128], replicated, may hold values from -3 to 3
Outputs:
- trunk_out: bfloat16 [1536, 8192], P('col', 'row')
- pair_out: bfloat16 [512, 128, 128], P('row', 'col')
All inputs are finite; a program needn't handle non-finite values.
Results may differ from a plain program's by a relative error of at most 0.012.
Values may be sent and summed in bfloat16 or wider, within the bound.
No kernel may reach another device: no remote copies, remote signals or barrier semaphores. Data moves between devices by JAX's collectives and lax.ppermute only.
A program may use at most 64 MiB of HBM per device.

v0:
```python
import jax
import jax.numpy as jnp
from jax import lax
from jax.sharding import PartitionSpec as P

TRUNK_CHANNELS = 1536
DILATION_STEP = 8
POOL = 16
OPM = 32
WINDOWS = 4
EPSILON = 1e-05


def with_halo(cells, sides, width):
    for axis, dim in sides:
        count = lax.axis_size(axis)
        ends = count - 1
        head = lax.slice_in_dim(cells, 0, width, axis=dim)
        tail = lax.slice_in_dim(cells, cells.shape[dim] - width, cells.shape[dim], axis=dim)
        cells = jnp.concatenate(
            [
                lax.ppermute(tail, axis, [(i, (i + 1) % count) for i in range(ends)]),
                cells,
                lax.ppermute(head, axis, [((i + 1) % count, i) for i in range(ends)]),
            ],
            axis=dim,
        )
    return cells


def partner_2(block, axis, bit):
    count = lax.axis_size(axis)
    route = []
    for low in range(count):
        high = low | 1 << bit
        if high != low and high < count:
            route += [(low, high), (high, low)]
    return lax.ppermute(block, axis, route)


def per_device(
    trunk_in, conv_weight, conv_bias, norm_gain, pair_proj, pair_in, opm_weight, pair_bias
):
    local_channels = trunk_in.shape[0]
    token_positions = trunk_in.shape[1]
    kernel = conv_weight.shape[0]
    border_width = 2 * DILATION_STEP
    per_window = lax.axis_size("row") // WINDOWS
    row_index = lax.axis_index("row")
    col_index = lax.axis_index("col")
    in_window = row_index % per_window
    source = trunk_in.astype(jnp.float32)
    zero_sum = jnp.zeros((local_channels, token_positions), jnp.float32)
    squares = lax.psum(jnp.sum(source * source, axis=0), "col")
    scale = lax.rsqrt(squares / TRUNK_CHANNELS + EPSILON)[None, :]
    own_gain = lax.dynamic_slice_in_dim(norm_gain, col_index * local_channels, local_channels, 0)
    gelu_output = jax.nn.gelu(source * own_gain[:, None] * scale).astype(jnp.bfloat16)
    padded_trunk = with_halo(gelu_output, (("row", 1),), border_width)
    carried = zero_sum
    piece = lax.all_gather(padded_trunk, "col", axis=0, tiled=True)
    for tap_offset in range(kernel):
        carried = carried + jnp.dot(
            conv_weight[tap_offset],
            piece[:, tap_offset * DILATION_STEP : tap_offset * DILATION_STEP + token_positions],
            preferred_element_type=jnp.float32,
        )
    trunk_out = (source + carried + conv_bias[:, None]).astype(jnp.bfloat16)
    pooled = (
        trunk_out.astype(jnp.float32)
        .reshape(local_channels, token_positions // POOL, POOL)
        .mean(axis=2)
        .astype(jnp.bfloat16)
    )
    own_proj = lax.dynamic_slice_in_dim(pair_proj, col_index * local_channels, local_channels, 1)
    pooled_f = pooled.astype(jnp.float32)
    partial_proj = lax.dot_general(
        pooled, own_proj, (((0,), (1,)), ((), ())), preferred_element_type=jnp.float32
    )
    projected, sums = lax.psum((partial_proj, jnp.sum(pooled_f * pooled_f, axis=0)), "col")
    sides = (projected * lax.rsqrt(sums / TRUNK_CHANNELS + EPSILON)[:, None]).astype(jnp.bfloat16)
    row_side = sides[:, :OPM]
    collected = sides[:, OPM:]
    col_block = pair_in.shape[1]
    pooled_rows = row_side.shape[0]
    for bit_num in range(per_window.bit_length() - 1):
        partner = partner_2(collected, "row", bit_num)
        upper_half = in_window // 2**bit_num % 2 == 1
        collected = jnp.where(
            upper_half,
            jnp.concatenate([partner, collected], axis=0),
            jnp.concatenate([collected, partner], axis=0),
        )
    own_cols = lax.dynamic_slice_in_dim(collected, col_index * col_block, col_block, 0)
    outer = (
        row_side.astype(jnp.float32)[:, None, :, None]
        * own_cols.astype(jnp.float32)[None, :, None, :]
    ).astype(jnp.bfloat16)
    outer = outer.reshape(pooled_rows * col_block, OPM * OPM)
    update = jnp.dot(outer, opm_weight, preferred_element_type=jnp.float32).reshape(pair_in.shape)
    pair_out = (pair_in.astype(jnp.float32) + update + pair_bias).astype(jnp.bfloat16)
    return (trunk_out, pair_out)


def solution(mesh):
    return jax.shard_map(
        per_device,
        mesh=mesh,
        in_specs=(
            P("col", "row"),
            P(None, "col", None),
            P("col"),
            P(),
            P(),
            P("row", "col", None),
            P(),
            P(),
        ),
        out_specs=(P("col", "row"), P("row", "col", None)),
        check_vma=False,
    )
```

profile of v0, /device:TPU:0, one launch (start us, length us, event | category | flops | bytes accessed | tf_op | source)
XLA Modules:
  0.0 115.7 jit_solution(4807338806114271744)
XLA Ops:
  7.2 0.0 copy-start
  7.2 0.0 all-gather.2.cloned.1.call-start
  7.2 1.5 %copy.25 = bf16[384,1024]{0,1:T(8,128)(2,1)S(1)} copy(bf16[384,1024]{1,0:T(8,128)(2,1)} %param.8) | data formatting | bytes 1572864 | tf_op args[0]
  8.8 0.2 fusion.21
  9.0 11.4 %psum.21 = f32[1024]{0:T(1024)S(1)} all-reduce(f32[1024]{0:T(1024)S(1)} %fusion.21), channel_id=1, replica_groups=mesh['row'=8,'col'=4] {'col'}, use_global_device_ids=true, to_apply=%region_1.2 | all-reduce | flops 1024 | bytes 8192 | tf_op jit(solution)/shard_map/psum | solution.py:54
  20.4 0.8 dynamic_slice.9
  21.2 0.7 fusion.16
  21.9 1.3 %collective-permute-start = (bf16[384,16]{0,1:T(8,128)(2,1)S(1)}, bf16[384,16]{0,1:T(8,128)(2,1)S(1)}, u32[]{:S(2)}, u32[]{:S(2)}) collective-permute-start(bf16[384,16]{0,1:T(8,128)(2,1)S(1)} %get-tuple-element.12), channel_id=1, source_target_pairs={{0,4},{4,8},{8,12},{12,16},{16,20},{20,24},{24,28},{1,5},{5,9},{9,... | collective-permute-start | bytes 36872 | tf_op jit(solution)/shard_map/ppermute | solution.py:22
  23.2 1.3 %collective-permute-start.1 = (bf16[384,16]{0,1:T(8,128)(2,1)S(1)}, bf16[384,16]{0,1:T(8,128)(2,1)S(1)}, u32[]{:S(2)}, u32[]{:S(2)}) collective-permute-start(bf16[384,16]{0,1:T(8,128)(2,1)S(1)} %get-tuple-element.13), channel_id=1, source_target_pairs={{4,0},{8,4},{12,8},{16,12},{20,16},{24,20},{28,24},{5,1},{9,5},{13... | collective-permute-start | bytes 36872 | tf_op jit(solution)/shard_map/ppermute | solution.py:24
  24.5 3.6 %collective-permute-done.1 = bf16[384,16]{0,1:T(8,128)(2,1)S(1)} collective-permute-done((bf16[384,16]{0,1:T(8,128)(2,1)S(1)}, bf16[384,16]{0,1:T(8,128)(2,1)S(1)}, u32[]{:S(2)}, u32[]{:S(2)}) %collective-permute-start.1) | collective-permute-done | bytes 12320 | tf_op jit(solution)/shard_map/ppermute | solution.py:24
  28.1 1.0 pad_maximum_fusion
  29.1 0.0 all-gather.2.cloned.1.call-update
  29.1 45.1 %all-gather.2.cloned.1.call-done = bf16[1536,1056]{0,1:T(8,128)(2,1)} async-done(((bf16[384,1056]{0,1:T(8,128)(2,1)}), bf16[1536,1056]{0,1:T(8,128)(2,1)}) %all-gather.2.cloned.1.call-update) | async-done | bytes 3244048 | tf_op jit(solution)/shard_map/all_gather | solution.py:60
  74.2 4.2 %fusion.5 = f32[1024,384]{1,0:T(8,128)S(1)} fusion(bf16[1536,1056]{0,1:T(8,128)(2,1)} %all-gather.2.cloned.1.call-done, bf16[5,384,1536]{2,1,0:T(8,128)(2,1)} %param.9), kind=kOutput, calls=%fused_computation.6 | convolution fusion | flops 1207959552 | bytes 5898240 | tf_op jit(solution)/shard_map/dot_general | solution.py:62
  78.4 0.0 slice-start.1
  78.4 3.2 %fusion.7 = f32[1024,384]{1,0:T(8,128)S(1)} fusion(bf16[1536,1056]{0,1:T(8,128)(2,1)S(1)} %copy-done.1, bf16[5,384,1536]{2,1,0:T(8,128)(2,1)} %param.9), kind=kOutput, calls=%fused_computation.8 | convolution fusion | flops 1207959552 | bytes 5898240 | tf_op jit(solution)/shard_map/dot_general | solution.py:62
  81.6 1.8 %fusion.9 = f32[1024,384]{1,0:T(8,128)S(1)} fusion(bf16[1536,1056]{0,1:T(8,128)(2,1)S(1)} %copy-done.1, bf16[5,384,1536]{2,1,0:T(8,128)(2,1)S(1)} %bitcast.28), kind=kOutput, calls=%fused_computation.10 | convolution fusion | flops 1207959552 | bytes 5898240 | tf_op jit(solution)/shard_map/dot_general | solution.py:62
  83.4 0.0 copy-start.3
  83.5 1.8 %fusion.11 = f32[1024,384]{1,0:T(8,128)S(1)} fusion(bf16[1536,1056]{0,1:T(8,128)(2,1)S(1)} %copy-done.1, bf16[5,384,1536]{2,1,0:T(8,128)(2,1)S(1)} %bitcast.28), kind=kOutput, calls=%fused_computation.12 | convolution fusion | flops 1207959552 | bytes 5898240 | tf_op jit(solution)/shard_map/dot_general | solution.py:62
  85.3 2.2 %convert_reduce_fusion = (f32[384,64]{0,1:T(8,128)S(1)}, bf16[384,1024]{0,1:T(8,128)(2,1)S(1)}) fusion(f32[384]{0:T(512)S(1)} %copy-done.3, bf16[5,384,1536]{2,1,0:T(8,128)(2,1)S(1)} %bitcast.28, bf16[1536,1056]{0,1:T(8,128)(2,1)S(1)} %copy-done.1, f32[1024,384]{1,0:T(8,128)S(1)} %fusion.5, f32[1024,384]{1,0:T(8,128)S(1)} %fusion.7, ...), kind=kOutput, calls=%fused_computation.30 | convolution fusion | flops 1211867136 | bytes 12290048 | tf_op jit(solution)/shard_map/dot_general | solution.py:62
  87.5 0.1 multiply_reduce_fusion
  87.6 0.9 fusion.41
  88.6 15.8 %all-reduce = (f32[64,64]{0,1:T(8,128)S(1)}, f32[64]{0:T(128)S(1)}) all-reduce(f32[64,64]{0,1:T(8,128)S(1)} %fusion.41, f32[64]{0:T(128)S(1)} %multiply_reduce_fusion), channel_id=1, replica_groups=mesh['row'=8,'col'=4] {'col'}, use_global_device_ids=true, to_apply=%region_3.4 | all-reduce | flops 4160 | bytes 33280 | tf_op jit(solution)/shard_map/psum | solution.py:79
  104.4 0.1 collective-permute-start.2
  104.5 1.2 %copy.29 = bf16[384,1024]{1,0:T(8,128)(2,1)} copy(bf16[384,1024]{0,1:T(8,128)(2,1)S(1)} %get-tuple-element.17) | data formatting | bytes 1572864
  105.8 0.2 copy.27
  105.9 0.0 collective-permute-done.2
  106.0 0.1 fusion.44
  106.1 0.1 copy.28
  106.2 0.2 mul.102
  106.4 0.3 copy-done.2
  106.8 2.1 %fusion.29 = bf16[64,32,128]{2,1,0:T(8,128)(2,1)} fusion(f32[32,1024]{1,0:T(8,128)S(1)} %mul.102, f32[64,1024]{1,0:T(8,128)S(1)} %copy.27, bf16[64,32,128]{2,1,0:T(8,128)(2,1)S(1)} %copy-done.2, f32[128]{0:T(128)S(1)} %copy-done.4, bf16[1024,128]{1,0:T(8,128)(2,1)S(1)} %copy-done), kind=kOutput, calls=%fused_computation.33 | convolution fusion | flops 542113792 | bytes 1704448 | tf_op jit(solution)/shard_map/dot_general | solution.py:99
  (19 shorter events, 0.1 us)
Async XLA Ops:
  7.2 99.3 %copy-start = (bf16[1024,128]{1,0:T(8,128)(2,1)S(1)}, bf16[1024,128]{1,0:T(8,128)(2,1)}, u32[]{:S(2)}) copy-start(bf16[1024,128]{1,0:T(8,128)(2,1)} %param.14) | copy-start | bytes 786436
  7.2 67.0 %all-gather.2.cloned.1.call-start = ((), (), s32[]{:S(2)}) async-start(), calls=%async_computation | async-start | bytes 4055040 | tf_op jit(solution)/shard_map/all_gather | solution.py:60
  21.9 2.6 %collective-permute-start = (bf16[384,16]{0,1:T(8,128)(2,1)S(1)}, bf16[384,16]{0,1:T(8,128)(2,1)S(1)}, u32[]{:S(2)}, u32[]{:S(2)}) collective-permute-start(bf16[384,16]{0,1:T(8,128)(2,1)S(1)} %get-tuple-element.12), channel_id=1, source_target_pairs={{0,4},{4,8},{8,12},{12,16},{16,20},{20,24},{24,28},{1,5},{5,9},{9,... | collective-permute-start | bytes 36872 | tf_op jit(solution)/shard_map/ppermute | solution.py:22
  23.2 4.9 %collective-permute-start.1 = (bf16[384,16]{0,1:T(8,128)(2,1)S(1)}, bf16[384,16]{0,1:T(8,128)(2,1)S(1)}, u32[]{:S(2)}, u32[]{:S(2)}) collective-permute-start(bf16[384,16]{0,1:T(8,128)(2,1)S(1)} %get-tuple-element.13), channel_id=1, source_target_pairs={{4,0},{8,4},{12,8},{16,12},{20,16},{24,20},{28,24},{5,1},{9,5},{13... | collective-permute-start | bytes 36872 | tf_op jit(solution)/shard_map/ppermute | solution.py:24
  74.2 4.2 %copy-start.1 = (bf16[1536,1056]{0,1:T(8,128)(2,1)S(1)}, bf16[1536,1056]{0,1:T(8,128)(2,1)}, u32[]{:S(2)}) copy-start(bf16[1536,1056]{0,1:T(8,128)(2,1)} %all-gather.2.cloned.1.call-done) | copy-start | bytes 9732100
  74.2 7.4 %slice-start = ((s8[5898240]{0:T(1024)(128)(4,1)}), s8[4194304]{0:T(1024)(128)(4,1)S(1)}, s32[]{:S(2)}) async-start(s8[5898240]{0:T(1024)(128)(4,1)} %bitcast.27), calls=%async_computation.1 | async-start | bytes 8388608
  78.4 3.2 %slice-start.1 = ((s8[5898240]{0:T(1024)(128)(4,1)}), s8[1703936]{0:T(1024)(128)(4,1)S(1)}, s32[]{:S(2)}) async-start(s8[5898240]{0:T(1024)(128)(4,1)} %bitcast.27), calls=%async_computation.2 | async-start | bytes 3407872
  83.4 1.8 %copy-start.3 = (f32[384]{0:T(512)S(1)}, f32[384]{0:T(512)}, u32[]{:S(2)}) copy-start(f32[384]{0:T(512)} %param.10) | copy-start | bytes 4612
  104.4 1.5 %collective-permute-start.2 = (bf16[64,32]{0,1:T(8,128)(2,1)S(1)}, bf16[64,32]{0,1:T(8,128)(2,1)S(1)}, u32[]{:S(2)}, u32[]{:S(2)}) collective-permute-start(bf16[64,32]{0,1:T(8,128)(2,1)S(1)} %get-tuple-element.15), channel_id=1, source_target_pairs={{0,4},{4,0},{8,12},{12,8},{16,20},{20,16},{24,28},{28,24},{1,5},{5... | collective-permute-start | bytes 12296 | tf_op jit(solution)/shard_map/ppermute | solution.py:38
  105.7 1.0 copy-start.2
  105.7 1.0 copy-start.4
Sparse Core Ops, SparseCore 0:
  29.2 44.9 all-gather.1
where the time goes:
time: 116 us
  waiting for transfers between devices  48.7 us (42%)
  blocking collectives  27.2 us (23%)
  matrix products  16.2 us (14%)
  between operations  14.3 us (12%)
  local copies, waits for them, and re-layouts  4.39 us (4%)
  starting transfers between devices  2.69 us (2%)
  other arithmetic  2.16 us (2%)
    all_gather x1, waiting for transfers between devices, per_device(): piece = lax.all_gather(padded_trunk, 'col', axis=0, tiled=True)  45.1 us
    psum x1, blocking collectives, per_device(): lax.psum((partial_proj, jnp.sum(pooled_f * pooled_f, axis=0)), 'col')  15.8 us
    dot_general x5, matrix products, per_device(): jnp.dot(conv_weight[tap_offset], piece[:, tap_offset * DILATION_STEP:tap_...  13.2 us
    psum x1, blocking collectives, per_device(): squares = lax.psum(jnp.sum(source * source, axis=0), 'col')  11.4 us
    ppermute x1, waiting for transfers between devices, with_halo(): lax.ppermute(head, axis, [((i + 1) % count, i) for i in range(ends)])  3.57 us
    unnamed x16, local copies, waits for them, and re-layouts  3.06 us
  transfers between devices with their start and end apart: 4, of which 2 were waited for; matrix products, arithmetic and copies ran while one was open for 1% of the time, Pallas kernels for 0%

commit v1 on v0

--- a/solution.py
+++ b/solution.py
@@ -9,6 +9,18 @@
 OPM = 32
 WINDOWS = 4
 EPSILON = 1e-05
+
+
+def collect(x, axis, dim):
+    ways, here = (lax.axis_size(axis), lax.axis_index(axis))
+    grown, reach = (x, 1)
+    while reach < ways:
+        theirs = lax.ppermute(grown, axis, [(d, d ^ reach) for d in range(ways)])
+        mine_first = jnp.concatenate([grown, theirs], axis=dim)
+        theirs_first = jnp.concatenate([theirs, grown], axis=dim)
+        grown = jnp.where(here & reach == 0, mine_first, theirs_first)
+        reach = 2 * reach
+    return grown
 
 
 def with_halo(cells, sides, width):
@@ -57,7 +69,7 @@
     gelu_output = jax.nn.gelu(source * own_gain[:, None] * scale).astype(jnp.bfloat16)
     padded_trunk = with_halo(gelu_output, (("row", 1),), border_width)
     carried = zero_sum
-    piece = lax.all_gather(padded_trunk, "col", axis=0, tiled=True)
+    piece = collect(padded_trunk, "col", 0)
     for tap_offset in range(kernel):
         carried = carried + jnp.dot(
             conv_weight[tap_offset],

time: 116 us -> 118 us (1.017)
  between operations: 14.3 us -> 0.91 us
  waiting for transfers between devices: 48.7 us -> 60.7 us
  other arithmetic: 2.16 us -> 8.04 us
  matrix products: 16.2 us -> 13.9 us
    ppermute x0 -> x2, waiting for transfers between devices: none -> 57.1 us  [collect(): theirs = lax.ppermute(grown, axis, [(d, d ^ reach) for d in range(ways)])]
    all_gather x1 -> x0, waiting for transfers between devices: 45.1 us -> none  [per_device(): piece = lax.all_gather(padded_trunk, 'col', axis=0, tiled=True)]
    select_n x0 -> x2, other arithmetic: none -> 6.79 us  [collect(): grown = jnp.where(here & reach == 0, mine_first, theirs_first)]
    dot_general x5, matrix products: 13.2 us -> 10.9 us  [per_device(): jnp.dot(conv_weight[tap_offset], piece[:, tap_offset * DILATION_STEP:tap_...]
    unnamed x16 -> x14, local copies, waits for them, and re-layouts: 3.06 us -> 3.06 us
  transfers between devices with their start and end apart: 4 -> 5, of which waited for: 2 -> 3; matrix products, arithmetic and copies ran while one was open for 1% -> 1% of each run, Pallas kernels for 0% -> 0%
where the time goes in v1:
time: 118 us; the launch traced here: 117 us
  waiting for transfers between devices  60.7 us (51%)
  blocking collectives  26.1 us (22%)
  matrix products  13.9 us (12%)
  other arithmetic  8.04 us (7%)
  local copies, waits for them, and re-layouts  4.4 us (4%)
  starting transfers between devices  3.36 us (3%)
    ppermute x2, waiting for transfers between devices, collect(): theirs = lax.ppermute(grown, axis, [(d, d ^ reach) for d in range(ways)])  57.1 us
    psum x1, blocking collectives, per_device(): lax.psum((partial_proj, jnp.sum(pooled_f * pooled_f, axis=0)), 'col')  14.7 us
    psum x1, blocking collectives, per_device(): squares = lax.psum(jnp.sum(source * source, axis=0), 'col')  11.4 us
    dot_general x5, matrix products, per_device(): jnp.dot(conv_weight[tap_offset], piece[:, tap_offset * DILATION_STEP:tap_...  10.9 us
    select_n x2, other arithmetic, collect(): grown = jnp.where(here & reach == 0, mine_first, theirs_first)  6.79 us
    ppermute x1, waiting for transfers between devices, with_halo(): lax.ppermute(head, axis, [((i + 1) % count, i) for i in range(ends)])  3.57 us
    unnamed x14, local copies, waits for them, and re-layouts  3.06 us
  transfers between devices with their start and end apart: 5, of which 3 were waited for; matrix products, arithmetic and copies ran while one was open for 1% of the time, Pallas kernels for 0%

profile of v1, /device:TPU:0, one launch (start us, length us, event | category | flops | bytes accessed | tf_op | source)
XLA Modules:
  0.0 117.3 jit_solution(9876173266557052427)
XLA Ops:
  0.6 0.0 copy-start
  0.6 1.5 %copy.25 = bf16[384,1024]{0,1:T(8,128)(2,1)S(1)} copy(bf16[384,1024]{1,0:T(8,128)(2,1)} %param.8) | data formatting | bytes 1572864 | tf_op args[0]
  2.2 0.2 fusion.21
  2.4 11.4 %psum.21 = f32[1024]{0:T(1024)S(1)} all-reduce(f32[1024]{0:T(1024)S(1)} %fusion.21), channel_id=1, replica_groups=mesh['row'=8,'col'=4] {'col'}, use_global_device_ids=true, to_apply=%region_1.2 | all-reduce | flops 1024 | bytes 8192 | tf_op jit(solution)/shard_map/psum | solution.py:66
  13.8 0.8 dynamic_slice.9
  14.6 0.7 fusion.16
  15.3 1.3 %collective-permute-start = (bf16[384,16]{0,1:T(8,128)(2,1)S(1)}, bf16[384,16]{0,1:T(8,128)(2,1)S(1)}, u32[]{:S(2)}, u32[]{:S(2)}) collective-permute-start(bf16[384,16]{0,1:T(8,128)(2,1)S(1)} %get-tuple-element.12), channel_id=1, source_target_pairs={{0,4},{4,8},{8,12},{12,16},{16,20},{20,24},{24,28},{1,5},{5,9},{9,... | collective-permute-start | bytes 36872 | tf_op jit(solution)/shard_map/ppermute | solution.py:34
  16.6 1.3 %collective-permute-start.1 = (bf16[384,16]{0,1:T(8,128)(2,1)S(1)}, bf16[384,16]{0,1:T(8,128)(2,1)S(1)}, u32[]{:S(2)}, u32[]{:S(2)}) collective-permute-start(bf16[384,16]{0,1:T(8,128)(2,1)S(1)} %get-tuple-element.13), channel_id=1, source_target_pairs={{4,0},{8,4},{12,8},{16,12},{20,16},{24,20},{28,24},{5,1},{9,5},{13... | collective-permute-start | bytes 36872 | tf_op jit(solution)/shard_map/ppermute | solution.py:36
  17.9 3.6 %collective-permute-done.1 = bf16[384,16]{0,1:T(8,128)(2,1)S(1)} collective-permute-done((bf16[384,16]{0,1:T(8,128)(2,1)S(1)}, bf16[384,16]{0,1:T(8,128)(2,1)S(1)}, u32[]{:S(2)}, u32[]{:S(2)}) %collective-permute-start.1) | collective-permute-done | bytes 12320 | tf_op jit(solution)/shard_map/ppermute | solution.py:36
  21.5 0.1 pad_maximum_fusion
  21.6 0.1 collective-permute-start.2
  21.7 19.6 %collective-permute-done.2 = bf16[384,1056]{0,1:T(8,128)(2,1)} collective-permute-done((bf16[384,1056]{0,1:T(8,128)(2,1)S(1)}, bf16[384,1056]{0,1:T(8,128)(2,1)}, u32[]{:S(2)}, u32[]{:S(2)}) %collective-permute-start.2) | collective-permute-done | bytes 811040 | tf_op jit(solution)/shard_map/ppermute | solution.py:18
  41.2 4.1 %maximum_select_fusion.1 = bf16[768,1056]{0,1:T(8,128)(2,1)S(1)} fusion(bf16[384,1056]{0,1:T(8,128)(2,1)} %collective-permute-done.2, bf16[384,16]{0,1:T(8,128)(2,1)S(1)} %collective-permute-done.1, bf16[384,1024]{0,1:T(8,128)(2,1)S(1)} %fusion.16, bf16[384,16]{0,1:T(8,128)(2,1)S(1)} %collective-permute-done, pred[]{:T(512)S(6)} %eq.13), kind=kLoop, calls=%fused_computation.19 | loop fusion | flops 13787136 | bytes 3244033 | tf_op jit(solution)/shard_map/jit(_where)/select_n | solution.py:21
  45.4 0.6 collective-permute-start.3
  46.0 37.5 %collective-permute-done.3 = bf16[768,1056]{0,1:T(8,128)(2,1)} collective-permute-done((bf16[768,1056]{0,1:T(8,128)(2,1)S(1)}, bf16[768,1056]{0,1:T(8,128)(2,1)}, u32[]{:S(2)}, u32[]{:S(2)}) %collective-permute-start.3) | collective-permute-done | bytes 1622048 | tf_op jit(solution)/shard_map/ppermute | solution.py:18
  83.5 2.6 %maximum_select_fusion = bf16[1536,1056]{0,1:T(8,128)(2,1)S(1)} fusion(bf16[768,1056]{0,1:T(8,128)(2,1)} %collective-permute-done.3, bf16[768,1056]{0,1:T(8,128)(2,1)S(1)} %maximum_select_fusion.1, pred[]{:T(512)S(6)} %eq.12), kind=kLoop, calls=%fused_computation.4 | loop fusion | flops 14598144 | bytes 6488065 | tf_op jit(solution)/shard_map/jit(_where)/select_n | solution.py:21
  86.2 3.2 %fusion.5 = f32[1024,384]{1,0:T(8,128)S(1)} fusion(bf16[1536,1056]{0,1:T(8,128)(2,1)S(1)} %maximum_select_fusion, bf16[5,384,1536]{2,1,0:T(8,128)(2,1)} %param.9), kind=kOutput, calls=%fused_computation.7 | convolution fusion | flops 1207959552 | bytes 5898240 | tf_op jit(solution)/shard_map/dot_general | solution.py:74
  89.4 1.8 %fusion.7 = f32[1024,384]{1,0:T(8,128)S(1)} fusion(bf16[1536,1056]{0,1:T(8,128)(2,1)S(1)} %maximum_select_fusion, bf16[5,384,1536]{2,1,0:T(8,128)(2,1)S(1)} %bitcast.30), kind=kOutput, calls=%fused_computation.9 | convolution fusion | flops 1207959552 | bytes 5898240 | tf_op jit(solution)/shard_map/dot_general | solution.py:74
  91.2 1.8 %fusion.9 = f32[1024,384]{1,0:T(8,128)S(1)} fusion(bf16[1536,1056]{0,1:T(8,128)(2,1)S(1)} %maximum_select_fusion, bf16[5,384,1536]{2,1,0:T(8,128)(2,1)S(1)} %bitcast.30), kind=kOutput, calls=%fused_computation.11 | convolution fusion | flops 1207959552 | bytes 5898240 | tf_op jit(solution)/shard_map/dot_general | solution.py:74
  93.1 1.8 %fusion.11 = f32[1024,384]{1,0:T(8,128)S(1)} fusion(bf16[1536,1056]{0,1:T(8,128)(2,1)S(1)} %maximum_select_fusion, bf16[5,384,1536]{2,1,0:T(8,128)(2,1)S(1)} %bitcast.30), kind=kOutput, calls=%fused_computation.13 | convolution fusion | flops 1207959552 | bytes 5898240 | tf_op jit(solution)/shard_map/dot_general | solution.py:74
  94.9 2.2 %convert_reduce_fusion = (f32[384,64]{0,1:T(8,128)S(1)}, bf16[384,1024]{0,1:T(8,128)(2,1)S(1)}) fusion(f32[384]{0:T(512)S(1)} %copy-done.2, bf16[5,384,1536]{2,1,0:T(8,128)(2,1)S(1)} %bitcast.30, bf16[1536,1056]{0,1:T(8,128)(2,1)S(1)} %maximum_select_fusion, f32[1024,384]{1,0:T(8,128)S(1)} %fusion.5, f32[1024,384]{1,0:T(8,128)S(1)} %fusion.7, ...), kind=kOutput, calls=%fused_computation.32 | convolution fusion | flops 1211867136 | bytes 12290048 | tf_op jit(solution)/shard_map/dot_general | solution.py:74
  97.1 0.1 multiply_reduce_fusion
  97.2 0.9 fusion.43
  98.2 14.7 %all-reduce = (f32[64,64]{0,1:T(8,128)S(1)}, f32[64]{0:T(128)S(1)}) all-reduce(f32[64,64]{0,1:T(8,128)S(1)} %fusion.43, f32[64]{0:T(128)S(1)} %multiply_reduce_fusion), channel_id=1, replica_groups=mesh['row'=8,'col'=4] {'col'}, use_global_device_ids=true, to_apply=%region_3.4 | all-reduce | flops 4160 | bytes 33280 | tf_op jit(solution)/shard_map/psum | solution.py:91
  112.9 0.1 collective-permute-start.4
  113.0 1.2 copy.29
  114.3 0.2 copy.27
  114.5 0.1 fusion.46
  114.6 0.1 copy.28
  114.7 0.2 mul.102
  114.9 0.3 copy-done.1
  115.3 2.1 %fusion.27 = bf16[64,32,128]{2,1,0:T(8,128)(2,1)} fusion(f32[32,1024]{1,0:T(8,128)S(1)} %mul.102, f32[64,1024]{1,0:T(8,128)S(1)} %copy.27, bf16[64,32,128]{2,1,0:T(8,128)(2,1)S(1)} %copy-done.1, f32[128]{0:T(128)S(1)} %copy-done.3, bf16[1024,128]{1,0:T(8,128)(2,1)S(1)} %copy-done), kind=kOutput, calls=%fused_computation.35 | convolution fusion | flops 542113792 | bytes 1704448 | tf_op jit(solution)/shard_map/dot_general | solution.py:111
  (20 shorter events, 0.1 us)
Async XLA Ops:
  0.6 114.3 %copy-start = (bf16[1024,128]{1,0:T(8,128)(2,1)S(1)}, bf16[1024,128]{1,0:T(8,128)(2,1)}, u32[]{:S(2)}) copy-start(bf16[1024,128]{1,0:T(8,128)(2,1)} %param.14) | copy-start | bytes 786436
  15.3 2.6 %collective-permute-start = (bf16[384,16]{0,1:T(8,128)(2,1)S(1)}, bf16[384,16]{0,1:T(8,128)(2,1)S(1)}, u32[]{:S(2)}, u32[]{:S(2)}) collective-permute-start(bf16[384,16]{0,1:T(8,128)(2,1)S(1)} %get-tuple-element.12), channel_id=1, source_target_pairs={{0,4},{4,8},{8,12},{12,16},{16,20},{20,24},{24,28},{1,5},{5,9},{9,... | collective-permute-start | bytes 36872 | tf_op jit(solution)/shard_map/ppermute | solution.py:34
  16.6 4.9 %collective-permute-start.1 = (bf16[384,16]{0,1:T(8,128)(2,1)S(1)}, bf16[384,16]{0,1:T(8,128)(2,1)S(1)}, u32[]{:S(2)}, u32[]{:S(2)}) collective-permute-start(bf16[384,16]{0,1:T(8,128)(2,1)S(1)} %get-tuple-element.13), channel_id=1, source_target_pairs={{4,0},{8,4},{12,8},{16,12},{20,16},{24,20},{28,24},{5,1},{9,5},{13... | collective-permute-start | bytes 36872 | tf_op jit(solution)/shard_map/ppermute | solution.py:36
  21.6 19.6 %collective-permute-start.2 = (bf16[384,1056]{0,1:T(8,128)(2,1)S(1)}, bf16[384,1056]{0,1:T(8,128)(2,1)}, u32[]{:S(2)}, u32[]{:S(2)}) collective-permute-start(bf16[384,1056]{0,1:T(8,128)(2,1)S(1)} %pad_maximum_fusion), channel_id=1, source_target_pairs={{0,1},{1,0},{2,3},{3,2},{4,5},{5,4},{6,7},{7,6},{8,9},{9,8},{10,11... | collective-permute-start | bytes 2433032 | tf_op jit(solution)/shard_map/ppermute | solution.py:18
  45.4 38.2 %collective-permute-start.3 = (bf16[768,1056]{0,1:T(8,128)(2,1)S(1)}, bf16[768,1056]{0,1:T(8,128)(2,1)}, u32[]{:S(2)}, u32[]{:S(2)}) collective-permute-start(bf16[768,1056]{0,1:T(8,128)(2,1)S(1)} %maximum_select_fusion.1), channel_id=1, source_target_pairs={{0,2},{1,3},{2,0},{3,1},{4,6},{5,7},{6,4},{7,5},{8,10},{9,11},{10,... | collective-permute-start | bytes 4866056 | tf_op jit(solution)/shard_map/ppermute | solution.py:18
  83.5 5.9 %slice-start = ((s8[5898240]{0:T(1024)(128)(4,1)}), s8[4194304]{0:T(1024)(128)(4,1)S(1)}, s32[]{:S(2)}) async-start(s8[5898240]{0:T(1024)(128)(4,1)} %bitcast.29), calls=%async_computation | async-start | bytes 8388608
  86.2 3.2 %slice-start.1 = ((s8[5898240]{0:T(1024)(128)(4,1)}), s8[1703936]{0:T(1024)(128)(4,1)S(1)}, s32[]{:S(2)}) async-start(s8[5898240]{0:T(1024)(128)(4,1)} %bitcast.29), calls=%async_computation.1 | async-start | bytes 3407872
  93.1 1.8 %copy-start.2 = (f32[384]{0:T(512)S(1)}, f32[384]{0:T(512)}, u32[]{:S(2)}) copy-start(f32[384]{0:T(512)} %param.10) | copy-start | bytes 4612
  112.9 1.5 %collective-permute-start.4 = (bf16[64,32]{0,1:T(8,128)(2,1)S(1)}, bf16[64,32]{0,1:T(8,128)(2,1)S(1)}, u32[]{:S(2)}, u32[]{:S(2)}) collective-permute-start(bf16[64,32]{0,1:T(8,128)(2,1)S(1)} %get-tuple-element.15), channel_id=1, source_target_pairs={{0,4},{4,0},{8,12},{12,8},{16,20},{20,16},{24,28},{28,24},{1,5},{5... | collective-permute-start | bytes 12296 | tf_op jit(solution)/shard_map/ppermute | solution.py:50
  114.2 1.0 copy-start.1
  114.2 1.0 copy-start.3
